TPU v7x, 128 devices: a whole 4x4x4 slice. The times are simulated.
128 devices in a mesh: section: 2 (over core), seq: 4 (over x), tensor: 16 (over z, y).
Axes of the slice: x: 4, y: 4, z: 4, core: 2. Of those that a mesh axis runs over, the one named last changes fastest.
Arguments:
- queries: bfloat16 [2560, 8192], P(('section', 'seq'), 'tensor'), may hold values from -200 to 200
- neighbours: bfloat16 [10240, 8192], P(('section', 'seq', 'tensor')), may hold values from -6 to 6
- kv_weight: bfloat16 [2, 8192, 8192], P(None, None, 'tensor'), may hold values from -0.0625 to 0.0625
- out_weight: bfloat16 [8192, 8192], P('tensor'), may hold values from -0.5 to 0.5
- slot_map: int32 [40], replicated, may hold values from 0 to 39, as said below
Outputs:
- mixed: bfloat16 [2560, 8192], P(('section', 'seq', 'tensor'))
Inputs may be any that keep to these rules, and one draw needn't show every extreme that they name: `slot_map`: distinct numbers; slot s lies on encoder shard s // 5; at most 2 spans of one sequence shard map to one encoder shard, and that many do for some pair of shards.
All inputs are finite; a program needn't handle non-finite values.
Results may differ from a plain program's by a relative error of at most 0.013.
Values may be sent and summed in bfloat16 or wider, within the bound.
No kernel may reach another device: no remote copies, remote signals or barrier semaphores. Data moves between devices by JAX's collectives and lax.ppermute only.
A program may use at most 128 MiB of HBM per device.

v0:
```python
import math
import jax
import jax.numpy as jnp
from jax import lax
from jax.sharding import PartitionSpec as P

HD = 128
SPAN = 64
PEER = 2
CH_DEV = 5
CAPC = 5
KEYS = 256


def attend(query_block, keys, values):
    scores = jnp.einsum("bqhd,bkhd->bhqk", query_block, keys, preferred_element_type=jnp.float32)
    scores = scores * (1.0 / math.sqrt(HD))
    peak = jnp.max(scores, axis=-1, keepdims=True)
    expo = jnp.exp(scores - peak)
    weights = (expo / jnp.sum(expo, axis=-1, keepdims=True)).astype(jnp.bfloat16)
    result = jnp.einsum("bhqk,bkhd->bqhd", weights, values, preferred_element_type=jnp.float32)
    return result.astype(jnp.bfloat16)


def on_device(queries, neighbours, kv_weight, out_weight, slot_map):
    groups = lax.axis_size(("section", "seq"))
    group_index = lax.axis_index(("section", "seq"))
    tensor_size = lax.axis_size("tensor")
    cols = kv_weight.shape[2]
    heads_local = cols // HD
    spans = slot_map.shape[0]
    rows_local = neighbours.shape[0]
    span_ids = jnp.arange(spans, dtype=jnp.int32)
    owner_shard = slot_map // CAPC
    slot_index = slot_map % CAPC
    seq_owner = span_ids // CH_DEV
    earlier = (seq_owner[:, None] == seq_owner[None, :]) & (
        owner_shard[:, None] == owner_shard[None, :]
    )
    earlier = earlier & (span_ids[None, :] < span_ids[:, None])
    arrival = jnp.sum(earlier.astype(jnp.int32), axis=1)
    peer_ids = jnp.arange(groups, dtype=jnp.int32)[:, None, None]
    place_ids = jnp.arange(PEER, dtype=jnp.int32)[None, :, None]
    own_spans = group_index * CH_DEV + jnp.arange(CH_DEV, dtype=jnp.int32)
    own_owner = owner_shard[own_spans]
    own_arrival = arrival[own_spans]
    pick_q = (own_owner[None, None, :] == peer_ids) & (own_arrival[None, None, :] == place_ids)
    send_q_idx = jnp.sum(
        jnp.where(pick_q, jnp.arange(CH_DEV, dtype=jnp.int32)[None, None, :], 0), axis=-1
    )
    query_blocks = queries.reshape(CH_DEV, SPAN, cols)
    send_q = query_blocks[send_q_idx]
    q_by_shift = [send_q[group_index]]
    for k in range(1, groups):
        block = lax.dynamic_index_in_dim(send_q, (group_index + k) % groups, 0, keepdims=False)
        pairs = [(s, (s + k) % groups) for s in range(groups)]
        q_by_shift.append(lax.ppermute(block, ("section", "seq"), pairs))
    recv_q = jnp.stack(q_by_shift)
    my_slots = group_index * CAPC + jnp.arange(CAPC, dtype=jnp.int32)
    hit = slot_map[None, :] == my_slots[:, None]
    slot_span = jnp.sum(jnp.where(hit, span_ids[None, :], 0), axis=1)
    slot_group = slot_span // CH_DEV
    slot_place = arrival[slot_span]
    q_for_slot = recv_q[(group_index - slot_group) % groups, slot_place]
    q_for_slot = q_for_slot.reshape(CAPC, SPAN, heads_local, HD)
    rows = lax.all_gather(neighbours, "tensor", axis=0, tiled=True)
    rows = rows.reshape(CAPC, KEYS, rows.shape[1])
    kv = jnp.einsum("skd,cde->cske", rows, kv_weight, preferred_element_type=jnp.float32)
    kv = kv.astype(jnp.bfloat16).reshape(2, CAPC, KEYS, heads_local, HD)
    keys, values = (kv[0], kv[1])
    attended = attend(q_for_slot, keys, values).reshape(CAPC, SPAN, cols)
    pick_a = (slot_group[None, None, :] == peer_ids) & (slot_place[None, None, :] == place_ids)
    send_a_idx = jnp.sum(
        jnp.where(pick_a, jnp.arange(CAPC, dtype=jnp.int32)[None, None, :], 0), axis=-1
    )
    send_a = attended[send_a_idx]
    by_shift = [send_a[group_index]]
    for k in range(1, groups):
        block = lax.dynamic_index_in_dim(send_a, (group_index + k) % groups, 0, keepdims=False)
        pairs = [(s, (s + k) % groups) for s in range(groups)]
        by_shift.append(lax.ppermute(block, ("section", "seq"), pairs))
    recv_a = jnp.stack(by_shift)
    shift_of = (group_index - own_owner) % groups
    attended_rows = recv_a[shift_of, own_arrival].reshape(tensor_size, -1, cols)
    partial = jnp.einsum(
        "srk,kn->srn", attended_rows, out_weight, preferred_element_type=jnp.float32
    ).astype(jnp.bfloat16)
    mixed = lax.psum_scatter(partial, "tensor", scatter_dimension=0, tiled=True)
    return mixed.reshape(-1, out_weight.shape[1])


def solution(mesh):
    placed = (
        P(("section", "seq"), "tensor"),
        P(("section", "seq", "tensor"), None),
        P(None, None, "tensor"),
        P("tensor", None),
        P(),
    )
    return jax.shard_map(
        on_device,
        mesh=mesh,
        in_specs=placed,
        out_specs=P(("section", "seq", "tensor"), None),
        check_vma=False,
    )
```

profile of v0, /device:TPU:0, one launch (start us, length us, event | category | flops | bytes accessed | tf_op | source)
XLA Modules:
  0.0 289.1 jit_solution(14220398571249133182)
XLA Ops:
  6.5 0.0 copy-start
  6.5 0.0 all-gather.2.cloned.1.call-start
  6.5 0.7 all-gather.2.cloned.1.call-update
  7.3 0.0 reduce-scatter.4.cloned.1.call-start
  7.5 0.6 gather_fusion
  8.1 0.2 convert_reduce_fusion
  8.3 0.7 gather_fusion.1
  9.0 0.2 select_reduce_fusion
  9.2 0.6 gather_fusion.3
  9.8 0.1 iota_compare_fusion.3
  9.9 0.1 iota_compare_fusion.4
  10.0 0.1 iota_compare_fusion.1
  10.0 0.1 iota_compare_fusion.2
  10.1 0.1 fusion.12
  10.2 0.1 copy.26
  10.3 0.1 reshape.388
  10.4 0.6 gather_fusion.2
  11.1 0.1 dynamic-slice_bitcast_fusion.7
  11.2 1.7 collective-permute-start
  12.9 2.7 collective-permute-start.1
  15.6 0.6 collective-permute-start.2
  16.2 0.7 collective-permute-start.3
  16.9 0.5 collective-permute-start.4
  17.4 0.1 copy.31
  17.4 0.1 reshape.410
  17.5 0.9 collective-permute-done
  18.4 0.2 collective-permute-start.5
  18.6 1.9 collective-permute-done.1
  20.5 0.2 collective-permute-start.6
  20.7 0.7 collective-permute-done.2
  21.4 0.0 collective-permute-done.3
  21.4 4.2 %collective-permute-done.4 = bf16[2,64,512]{2,1,0:T(8,128)(2,1)S(1)} collective-permute-done((bf16[2,64,512]{2,1,0:T(8,128)(2,1)S(1)}, bf16[2,64,512]{2,1,0:T(8,128)(2,1)S(1)}, u32[]{:S(2)}, u32[]{:S(2)}) %collective-permute-start.4) | collective-permute-done | bytes 131104 | tf_op jit(solution)/shard_map/ppermute | solution.py:57
  25.7 1.7 collective-permute-done.5
  27.3 0.2 collective-permute-done.6
  27.5 0.6 gather_fusion.4
  28.1 116.7 %all-gather.2.cloned.1.call-done = bf16[1280,8192]{1,0:T(8,128)(2,1)} async-done(((bf16[80,8192]{1,0:T(8,128)(2,1)}), bf16[1280,8192]{1,0:T(8,128)(2,1)}) %all-gather.2.cloned.1.call-update) | async-done | bytes 20971536 | tf_op jit(solution)/shard_map/all_gather | solution.py:66
  144.8 26.7 %convert_bitcast_fusion = bf16[2,5,256,512]{2,3,1,0:T(8,128)(2,1)S(1)} fusion(bf16[5,256,8192,1]{2,1,0,3:T(8,128)(2,1)} %bitcast.146, bf16[2,8192,512]{2,1,0:T(8,128)(2,1)} %param.7), kind=kOutput, calls=%fused_computation.12 | convolution fusion | flops 21476147200 | bytes 40370176 | tf_op jit(solution)/shard_map/skd,cde->cske/dot_general | solution.py:68
  171.5 0.2 fusion.32
  171.7 0.3 convolution_multiply_fusion
  172.0 0.4 fusion.33
  172.4 2.3 fusion.8
  174.7 0.1 copy.44
  174.8 0.6 gather_fusion.5
  175.4 0.1 dynamic-slice_bitcast_fusion
  175.6 1.5 collective-permute-start.7
  177.1 2.8 collective-permute-start.8
  179.9 0.5 collective-permute-start.9
  180.3 0.8 collective-permute-start.10
  181.2 0.5 collective-permute-start.11
  181.6 1.9 collective-permute-done.7
  183.6 0.0 collective-permute-start.12
  183.6 0.9 collective-permute-done.8
  184.5 0.9 collective-permute-start.13
  185.4 0.4 collective-permute-done.9
  185.8 0.0 collective-permute-done.10
  185.8 5.7 %collective-permute-done.11 = bf16[2,64,512]{2,1,0:T(8,128)(2,1)S(1)} collective-permute-done((bf16[2,64,512]{2,1,0:T(8,128)(2,1)S(1)}, bf16[2,64,512]{2,1,0:T(8,128)(2,1)S(1)}, u32[]{:S(2)}, u32[]{:S(2)}) %collective-permute-start.11) | collective-permute-done | bytes 131104 | tf_op jit(solution)/shard_map/ppermute | solution.py:81
  191.5 0.0 collective-permute-done.12
  191.5 0.0 collective-permute-done.13
  191.6 0.6 gather_fusion.6
  192.2 0.1 reshape.368
  192.2 8.7 %convolution_convert_fusion = bf16[16,20,8192]{2,1,0:T(8,128)(2,1)} fusion(bf16[16,20,512]{2,1,0:T(8,128)(2,1)S(1)} %reshape.368, bf16[512,8192]{1,0:T(8,128)(2,1)} %param.8), kind=kOutput, calls=%fused_computation.10 | convolution fusion | flops 2686976000 | bytes 13959168 | tf_op jit(solution)/shard_map/srk,kn->srn/dot_general | solution.py:85
  200.9 0.0 reduce-scatter.4.cloned.1.call-update
  201.0 0.0 copy-start.1
  201.0 81.3 %reduce-scatter.4.cloned.1.call-done = bf16[1,20,8192]{2,1,0:T(8,128)(2,1)} async-done(((bf16[16,20,8192]{2,1,0:T(8,128)(2,1)}), bf16[1,20,8192]{2,1,0:T(8,128)(2,1)}) %reduce-scatter.4.cloned.1.call-update) | async-done | bytes 327696
  (32 shorter events, 0.3 us)
Async XLA Ops:
  6.5 3.9 %copy-start = (bf16[320,512]{1,0:T(8,128)(2,1)S(1)}, bf16[320,512]{1,0:T(8,128)(2,1)}, u32[]{:S(2)}) copy-start(bf16[320,512]{1,0:T(8,128)(2,1)} %param.5) | copy-start | bytes 983044
  6.5 0.9 copy-start.2
  6.5 138.2 %all-gather.2.cloned.1.call-start = ((), (), s32[]{:S(2)}) async-start(), calls=%async_computation.1 | async-start | bytes 22282240 | tf_op jit(solution)/shard_map/all_gather | solution.py:66
  7.3 275.0 %reduce-scatter.4.cloned.1.call-start = ((), (), s32[]{:S(2)}) async-start(), calls=%async_computation.2 | async-start | bytes 6684672
  11.2 7.2 %collective-permute-start = (bf16[2,64,512]{2,1,0:T(8,128)(2,1)S(1)}, bf16[2,64,512]{2,1,0:T(8,128)(2,1)S(1)}, u32[]{:S(2)}, u32[]{:S(2)}) collective-permute-start(bf16[2,64,512]{2,1,0:T(8,128)(2,1)S(1)} %get-tuple-element.21), channel_id=1, source_target_pairs={{0,16},{16,32},{32,48},{48,64},{64,80},{80,96},{96,112},{112,0},{1... | collective-permute-start | bytes 393224 | tf_op jit(solution)/shard_map/ppermute | solution.py:57
  12.9 7.6 %collective-permute-start.1 = (bf16[2,64,512]{2,1,0:T(8,128)(2,1)S(1)}, bf16[2,64,512]{2,1,0:T(8,128)(2,1)S(1)}, u32[]{:S(2)}, u32[]{:S(2)}) collective-permute-start(bf16[2,64,512]{2,1,0:T(8,128)(2,1)S(1)} %get-tuple-element.20), channel_id=1, source_target_pairs={{0,32},{16,48},{32,64},{48,80},{64,96},{80,112},{96,0},{112,16},{1... | collective-permute-start | bytes 393224 | tf_op jit(solution)/shard_map/ppermute | solution.py:57
  15.6 5.8 %collective-permute-start.2 = (bf16[2,64,512]{2,1,0:T(8,128)(2,1)S(1)}, bf16[2,64,512]{2,1,0:T(8,128)(2,1)S(1)}, u32[]{:S(2)}, u32[]{:S(2)}) collective-permute-start(bf16[2,64,512]{2,1,0:T(8,128)(2,1)S(1)} %get-tuple-element.19), channel_id=1, source_target_pairs={{0,48},{16,64},{32,80},{48,96},{64,112},{80,0},{96,16},{112,32},{1... | collective-permute-start | bytes 393224 | tf_op jit(solution)/shard_map/ppermute | solution.py:57
  16.2 5.2 %collective-permute-start.3 = (bf16[2,64,512]{2,1,0:T(8,128)(2,1)S(1)}, bf16[2,64,512]{2,1,0:T(8,128)(2,1)S(1)}, u32[]{:S(2)}, u32[]{:S(2)}) collective-permute-start(bf16[2,64,512]{2,1,0:T(8,128)(2,1)S(1)} %get-tuple-element.18), channel_id=1, source_target_pairs={{0,64},{16,80},{32,96},{48,112},{64,0},{80,16},{96,32},{112,48},{1... | collective-permute-start | bytes 393224 | tf_op jit(solution)/shard_map/ppermute | solution.py:57
  16.9 8.8 %collective-permute-start.4 = (bf16[2,64,512]{2,1,0:T(8,128)(2,1)S(1)}, bf16[2,64,512]{2,1,0:T(8,128)(2,1)S(1)}, u32[]{:S(2)}, u32[]{:S(2)}) collective-permute-start(bf16[2,64,512]{2,1,0:T(8,128)(2,1)S(1)} %get-tuple-element.17), channel_id=1, source_target_pairs={{0,80},{16,96},{32,112},{48,0},{64,16},{80,32},{96,48},{112,64},{1... | collective-permute-start | bytes 393224 | tf_op jit(solution)/shard_map/ppermute | solution.py:57
  18.4 8.9 %collective-permute-start.5 = (bf16[2,64,512]{2,1,0:T(8,128)(2,1)S(1)}, bf16[2,64,512]{2,1,0:T(8,128)(2,1)S(1)}, u32[]{:S(2)}, u32[]{:S(2)}) collective-permute-start(bf16[2,64,512]{2,1,0:T(8,128)(2,1)S(1)} %get-tuple-element.16), channel_id=1, source_target_pairs={{0,96},{16,112},{32,0},{48,16},{64,32},{80,48},{96,64},{112,80},{1... | collective-permute-start | bytes 393224 | tf_op jit(solution)/shard_map/ppermute | solution.py:57
  20.5 7.1 %collective-permute-start.6 = (bf16[2,64,512]{2,1,0:T(8,128)(2,1)S(1)}, bf16[2,64,512]{2,1,0:T(8,128)(2,1)S(1)}, u32[]{:S(2)}, u32[]{:S(2)}) collective-permute-start(bf16[2,64,512]{2,1,0:T(8,128)(2,1)S(1)} %get-tuple-element.15), channel_id=1, source_target_pairs={{0,112},{16,0},{32,16},{48,32},{64,48},{80,64},{96,80},{112,96},{1... | collective-permute-start | bytes 393224 | tf_op jit(solution)/shard_map/ppermute | solution.py:57
  175.6 8.0 %collective-permute-start.7 = (bf16[2,64,512]{2,1,0:T(8,128)(2,1)S(1)}, bf16[2,64,512]{2,1,0:T(8,128)(2,1)S(1)}, u32[]{:S(2)}, u32[]{:S(2)}) collective-permute-start(bf16[2,64,512]{2,1,0:T(8,128)(2,1)S(1)} %get-tuple-element.13), channel_id=1, source_target_pairs={{0,16},{16,32},{32,48},{48,64},{64,80},{80,96},{96,112},{112,0},{1... | collective-permute-start | bytes 393224 | tf_op jit(solution)/shard_map/ppermute | solution.py:81
  177.1 7.4 %collective-permute-start.8 = (bf16[2,64,512]{2,1,0:T(8,128)(2,1)S(1)}, bf16[2,64,512]{2,1,0:T(8,128)(2,1)S(1)}, u32[]{:S(2)}, u32[]{:S(2)}) collective-permute-start(bf16[2,64,512]{2,1,0:T(8,128)(2,1)S(1)} %get-tuple-element.12), channel_id=1, source_target_pairs={{0,32},{16,48},{32,64},{48,80},{64,96},{80,112},{96,0},{112,16},{1... | collective-permute-start | bytes 393224 | tf_op jit(solution)/shard_map/ppermute | solution.py:81
  179.9 5.9 %collective-permute-start.9 = (bf16[2,64,512]{2,1,0:T(8,128)(2,1)S(1)}, bf16[2,64,512]{2,1,0:T(8,128)(2,1)S(1)}, u32[]{:S(2)}, u32[]{:S(2)}) collective-permute-start(bf16[2,64,512]{2,1,0:T(8,128)(2,1)S(1)} %get-tuple-element.11), channel_id=1, source_target_pairs={{0,48},{16,64},{32,80},{48,96},{64,112},{80,0},{96,16},{112,32},{1... | collective-permute-start | bytes 393224 | tf_op jit(solution)/shard_map/ppermute | solution.py:81
  180.3 5.5 %collective-permute-start.10 = (bf16[2,64,512]{2,1,0:T(8,128)(2,1)S(1)}, bf16[2,64,512]{2,1,0:T(8,128)(2,1)S(1)}, u32[]{:S(2)}, u32[]{:S(2)}) collective-permute-start(bf16[2,64,512]{2,1,0:T(8,128)(2,1)S(1)} %get-tuple-element.10), channel_id=1, source_target_pairs={{0,64},{16,80},{32,96},{48,112},{64,0},{80,16},{96,32},{112,48},{1... | collective-permute-start | bytes 393224 | tf_op jit(solution)/shard_map/ppermute | solution.py:81
  181.2 10.3 %collective-permute-start.11 = (bf16[2,64,512]{2,1,0:T(8,128)(2,1)S(1)}, bf16[2,64,512]{2,1,0:T(8,128)(2,1)S(1)}, u32[]{:S(2)}, u32[]{:S(2)}) collective-permute-start(bf16[2,64,512]{2,1,0:T(8,128)(2,1)S(1)} %get-tuple-element.9), channel_id=1, source_target_pairs={{0,80},{16,96},{32,112},{48,0},{64,16},{80,32},{96,48},{112,64},{1... | collective-permute-start | bytes 393224 | tf_op jit(solution)/shard_map/ppermute | solution.py:81
  183.6 8.0 %collective-permute-start.12 = (bf16[2,64,512]{2,1,0:T(8,128)(2,1)S(1)}, bf16[2,64,512]{2,1,0:T(8,128)(2,1)S(1)}, u32[]{:S(2)}, u32[]{:S(2)}) collective-permute-start(bf16[2,64,512]{2,1,0:T(8,128)(2,1)S(1)} %get-tuple-element.8), channel_id=1, source_target_pairs={{0,96},{16,112},{32,0},{48,16},{64,32},{80,48},{96,64},{112,80},{1... | collective-permute-start | bytes 393224 | tf_op jit(solution)/shard_map/ppermute | solution.py:81
  184.5 7.1 %collective-permute-start.13 = (bf16[2,64,512]{2,1,0:T(8,128)(2,1)S(1)}, bf16[2,64,512]{2,1,0:T(8,128)(2,1)S(1)}, u32[]{:S(2)}, u32[]{:S(2)}) collective-permute-start(bf16[2,64,512]{2,1,0:T(8,128)(2,1)S(1)} %get-tuple-element.7), channel_id=1, source_target_pairs={{0,112},{16,0},{32,16},{48,32},{64,48},{80,64},{96,80},{112,96},{1... | collective-permute-start | bytes 393224 | tf_op jit(solution)/shard_map/ppermute | solution.py:81
  201.0 81.3 %copy-start.1 = (bf16[320,512]{1,0:T(8,128)(2,1)S(1)}, bf16[320,512]{1,0:T(8,128)(2,1)}, u32[]{:S(2)}) copy-start(bf16[320,512]{1,0:T(8,128)(2,1)} %param.5) | copy-start | bytes 983044
Sparse Core Ops, SparseCore 0:
  9.5 135.2 all-gather.1
  201.1 81.1 reduce-scatter.3
where the time goes:
time: 289 us
  waiting for transfers between devices  217 us (75%)
  matrix products  38 us (13%)
  between operations  13.8 us (5%)
  starting transfers between devices  13.5 us (5%)
  local copies, waits for them, and re-layouts  5.33 us (2%)
    all_gather x1, waiting for transfers between devices, on_device(): rows = lax.all_gather(neighbours, 'tensor', axis=0, tiled=True)  117 us
    unnamed x3, waiting for transfers between devices  82 us
    dot_general x1, matrix products, on_device(): jnp.einsum('skd,cde->cske', rows, kv_weight, preferred_element_type=jnp.f...  26.7 us
    ppermute x7, waiting for transfers between devices, on_device(): q_by_shift.append(lax.ppermute(block, ('section', 'seq'), pairs))  9.52 us
    ppermute x7, waiting for transfers between devices, on_device(): by_shift.append(lax.ppermute(block, ('section', 'seq'), pairs))  8.93 us
    dot_general x1, matrix products, on_device(): jnp.einsum('srk,kn->srn', attended_rows, out_weight, preferred_element_ty...  8.7 us
    ppermute x7, starting transfers between devices, on_device(): by_shift.append(lax.ppermute(block, ('section', 'seq'), pairs))  6.93 us
    ppermute x7, starting transfers between devices, on_device(): q_by_shift.append(lax.ppermute(block, ('section', 'seq'), pairs))  6.53 us
  transfers between devices with their start and end apart: 16, of which 12 were waited for; matrix products, arithmetic and copies ran while one was open for 2% of the time, Pallas kernels for 0%

commit v1 on v0

--- a/solution.py
+++ b/solution.py
@@ -10,6 +10,12 @@
 CH_DEV = 5
 CAPC = 5
 KEYS = 256
+_list_values = lambda q_in: jnp.concatenate(
+    jax.lax.all_to_all(
+        jnp.stack([q_in for _ in range(jax.lax.axis_size("tensor"))], axis=0), "tensor", 0, 0
+    ),
+    0,
+)
 
 
 def attend(query_block, keys, values):
@@ -63,7 +69,7 @@
     slot_place = arrival[slot_span]
     q_for_slot = recv_q[(group_index - slot_group) % groups, slot_place]
     q_for_slot = q_for_slot.reshape(CAPC, SPAN, heads_local, HD)
-    rows = lax.all_gather(neighbours, "tensor", axis=0, tiled=True)
+    rows = _list_values(neighbours)
     rows = rows.reshape(CAPC, KEYS, rows.shape[1])
     kv = jnp.einsum("skd,cde->cske", rows, kv_weight, preferred_element_type=jnp.float32)
     kv = kv.astype(jnp.bfloat16).reshape(2, CAPC, KEYS, heads_local, HD)

time: 289 us -> 479 us (1.66)
  waiting for transfers between devices: 217 us -> 390 us
  starting transfers between devices: 13.5 us -> 22.2 us
  local copies, waits for them, and re-layouts: 5.33 us -> 13.6 us
    all_to_all x0 -> x1, waiting for transfers between devices: none -> 292 us  [jax.lax.all_to_all(jnp.stack([q_in for _ in range(jax.lax.axis_size('tens...]
    all_gather x1 -> x0, waiting for transfers between devices: 117 us -> none  [on_device(): rows = lax.all_gather(neighbours, 'tensor', axis=0, tiled=True)]
    all_to_all x0 -> x1, starting transfers between devices: none -> 8.34 us  [jax.lax.all_to_all(jnp.stack([q_in for _ in range(jax.lax.axis_size('tens...]
    another operation x0 -> x1, local copies, waits for them, and re-layouts: none -> 8.29 us  [jnp.stack([q_in for _ in range(jax.lax.axis_size('tensor'))], axis=0)]
    unnamed x3 -> x2, waiting for transfers between devices: 82 us -> 79.3 us
  transfers between devices with their start and end apart: 16 -> 16, of which waited for: 12 -> 12; matrix products, arithmetic and copies ran while one was open for 2% -> 1% of each run, Pallas kernels for 0% -> 0%
where the time goes in v1:
time: 479 us
  waiting for transfers between devices  390 us (81%)
  matrix products  38 us (8%)
  starting transfers between devices  22.2 us (5%)
  between operations  13.8 us (3%)
  local copies, waits for them, and re-layouts  13.6 us (3%)
    all_to_all x1, waiting for transfers between devices, jax.lax.all_to_all(jnp.stack([q_in for _ in range(jax.lax.axis_size('tens...  292 us
    unnamed x2, waiting for transfers between devices  79.3 us
    dot_general x1, matrix products, on_device(): jnp.einsum('skd,cde->cske', rows, kv_weight, preferred_element_type=jnp.f...  26.7 us
  transfers between devices with their start and end apart: 16, of which 12 were waited for; matrix products, arithmetic and copies ran while one was open for 1% of the time, Pallas kernels for 0%

profile of v1, /device:TPU:0, one launch (start us, length us, event | category | flops | bytes accessed | tf_op | source)
XLA Modules:
  0.0 478.6 jit_solution(17430976814937260755)
XLA Ops:
  6.5 0.0 copy-start
  6.5 8.3 %stack.67 = bf16[16,80,8192]{2,1,0:T(8,128)(2,1)} broadcast(bf16[80,8192]{1,0:T(8,128)(2,1)} %param.6), dimensions={1,2} | broadcast | bytes 22282240 | tf_op jit(solution)/shard_map/stack | solution.py:15
  14.8 8.3 %all-to-all-start = ((bf16[16,80,8192]{2,1,0:T(8,128)(2,1)}), bf16[16,80,8192]{2,1,0:T(8,128)(2,1)}, u32[]{:S(2)}, u32[]{:S(2)}) async-start(bf16[16,80,8192]{2,1,0:T(8,128)(2,1)} %stack.67), calls=%async_computation | async-start | bytes 41943040 | tf_op jit(solution)/shard_map/all_to_all | solution.py:14
  23.2 0.0 reduce-scatter.4.cloned.1.call-start
  23.4 0.6 gather_fusion
  24.0 0.2 convert_reduce_fusion
  24.2 0.7 gather_fusion.1
  24.9 0.2 select_reduce_fusion
  25.1 0.6 gather_fusion.3
  25.7 0.1 iota_compare_fusion.3
  25.8 0.1 iota_compare_fusion.4
  25.9 0.1 iota_compare_fusion.1
  26.0 0.1 iota_compare_fusion.2
  26.0 0.1 fusion.12
  26.1 0.1 copy.26
  26.2 0.1 reshape.386
  26.3 0.6 gather_fusion.2
  27.0 0.1 dynamic-slice_bitcast_fusion.7
  27.1 1.6 collective-permute-start
  28.6 2.7 collective-permute-start.1
  31.4 0.3 collective-permute-start.2
  31.7 1.0 collective-permute-start.3
  32.6 0.5 collective-permute-start.4
  33.1 0.1 copy.31
  33.2 0.1 reshape.408
  33.3 1.6 collective-permute-done
  35.0 0.0 collective-permute-start.5
  35.0 1.0 collective-permute-done.1
  35.9 0.8 collective-permute-start.6
  36.8 0.4 collective-permute-done.2
  37.2 0.0 collective-permute-done.3
  37.2 5.8 %collective-permute-done.4 = bf16[2,64,512]{2,1,0:T(8,128)(2,1)S(1)} collective-permute-done((bf16[2,64,512]{2,1,0:T(8,128)(2,1)S(1)}, bf16[2,64,512]{2,1,0:T(8,128)(2,1)S(1)}, u32[]{:S(2)}, u32[]{:S(2)}) %collective-permute-start.4) | collective-permute-done | bytes 131104 | tf_op jit(solution)/shard_map/ppermute | solution.py:63
  43.0 0.0 collective-permute-done.5
  43.0 0.1 collective-permute-done.6
  43.1 0.6 gather_fusion.4
  43.7 292.4 %all-to-all-done = bf16[16,80,8192]{2,1,0:T(8,128)(2,1)} async-done(((bf16[16,80,8192]{2,1,0:T(8,128)(2,1)}), bf16[16,80,8192]{2,1,0:T(8,128)(2,1)}, u32[]{:S(2)}, u32[]{:S(2)}) %all-to-all-start) | async-done | bytes 20971552 | tf_op jit(solution)/shard_map/all_to_all | solution.py:14
  336.1 26.7 %convert_bitcast_fusion = bf16[2,5,256,512]{2,3,1,0:T(8,128)(2,1)S(1)} fusion(bf16[5,256,8192,1]{2,1,0,3:T(8,128)(2,1)} %bitcast.2, bf16[2,8192,512]{2,1,0:T(8,128)(2,1)} %param.7), kind=kOutput, calls=%fused_computation.12 | convolution fusion | flops 21476147200 | bytes 40370176 | tf_op jit(solution)/shard_map/skd,cde->cske/dot_general | solution.py:74
  362.8 0.2 fusion.32
  363.0 0.3 convolution_multiply_fusion
  363.4 0.4 fusion.33
  363.8 2.3 fusion.8
  366.1 0.1 copy.44
  366.2 0.6 gather_fusion.5
  366.8 0.1 dynamic-slice_bitcast_fusion
  366.9 1.6 collective-permute-start.7
  368.5 2.8 collective-permute-start.8
  371.3 0.0 collective-permute-start.9
  371.3 1.3 collective-permute-start.10
  372.6 0.5 collective-permute-start.11
  373.0 1.7 collective-permute-done.7
  374.7 0.0 collective-permute-start.12
  374.7 1.1 collective-permute-done.8
  375.9 0.8 collective-permute-start.13
  376.7 0.4 collective-permute-done.9
  377.1 0.0 collective-permute-done.10
  377.1 5.7 %collective-permute-done.11 = bf16[2,64,512]{2,1,0:T(8,128)(2,1)S(1)} collective-permute-done((bf16[2,64,512]{2,1,0:T(8,128)(2,1)S(1)}, bf16[2,64,512]{2,1,0:T(8,128)(2,1)S(1)}, u32[]{:S(2)}, u32[]{:S(2)}) %collective-permute-start.11) | collective-permute-done | bytes 131104 | tf_op jit(solution)/shard_map/ppermute | solution.py:87
  382.9 0.0 collective-permute-done.12
  382.9 0.1 collective-permute-done.13
  383.0 0.6 gather_fusion.6
  383.6 0.1 reshape.366
  383.7 8.7 %convolution_convert_fusion = bf16[16,20,8192]{2,1,0:T(8,128)(2,1)} fusion(bf16[16,20,512]{2,1,0:T(8,128)(2,1)S(1)} %reshape.366, bf16[512,8192]{1,0:T(8,128)(2,1)} %param.8), kind=kOutput, calls=%fused_computation.10 | convolution fusion | flops 2686976000 | bytes 13959168 | tf_op jit(solution)/shard_map/srk,kn->srn/dot_general | solution.py:91
  392.4 0.0 reduce-scatter.4.cloned.1.call-update
  392.4 0.0 copy-start.1
  392.4 79.3 %reduce-scatter.4.cloned.1.call-done = bf16[1,20,8192]{2,1,0:T(8,128)(2,1)} async-done(((bf16[16,20,8192]{2,1,0:T(8,128)(2,1)}), bf16[1,20,8192]{2,1,0:T(8,128)(2,1)}) %reduce-scatter.4.cloned.1.call-update) | async-done | bytes 327696
  (32 shorter events, 0.3 us)
Async XLA Ops:
  6.5 19.8 %copy-start = (bf16[320,512]{1,0:T(8,128)(2,1)S(1)}, bf16[320,512]{1,0:T(8,128)(2,1)}, u32[]{:S(2)}) copy-start(bf16[320,512]{1,0:T(8,128)(2,1)} %param.5) | copy-start | bytes 983044
  14.8 8.5 %copy-start.2 = (s32[40]{0:T(128)S(1)}, s32[40]{0:T(128)}, u32[]{:S(2)}) copy-start(s32[40]{0:T(128)} %param.9) | copy-start | bytes 484
  14.8 321.3 %all-to-all-start = ((bf16[16,80,8192]{2,1,0:T(8,128)(2,1)}), bf16[16,80,8192]{2,1,0:T(8,128)(2,1)}, u32[]{:S(2)}, u32[]{:S(2)}) async-start(bf16[16,80,8192]{2,1,0:T(8,128)(2,1)} %stack.67), calls=%async_computation | async-start | bytes 41943040 | tf_op jit(solution)/shard_map/all_to_all | solution.py:14
  23.2 448.6 %reduce-scatter.4.cloned.1.call-start = ((), (), s32[]{:S(2)}) async-start(), calls=%async_computation.2 | async-start | bytes 6684672
  27.1 7.9 %collective-permute-start = (bf16[2,64,512]{2,1,0:T(8,128)(2,1)S(1)}, bf16[2,64,512]{2,1,0:T(8,128)(2,1)S(1)}, u32[]{:S(2)}, u32[]{:S(2)}) collective-permute-start(bf16[2,64,512]{2,1,0:T(8,128)(2,1)S(1)} %get-tuple-element.21), channel_id=1, source_target_pairs={{0,16},{16,32},{32,48},{48,64},{64,80},{80,96},{96,112},{112,0},{1... | collective-permute-start | bytes 393224 | tf_op jit(solution)/shard_map/ppermute | solution.py:63
  28.6 7.3 %collective-permute-start.1 = (bf16[2,64,512]{2,1,0:T(8,128)(2,1)S(1)}, bf16[2,64,512]{2,1,0:T(8,128)(2,1)S(1)}, u32[]{:S(2)}, u32[]{:S(2)}) collective-permute-start(bf16[2,64,512]{2,1,0:T(8,128)(2,1)S(1)} %get-tuple-element.20), channel_id=1, source_target_pairs={{0,32},{16,48},{32,64},{48,80},{64,96},{80,112},{96,0},{112,16},{1... | collective-permute-start | bytes 393224 | tf_op jit(solution)/shard_map/ppermute | solution.py:63
  31.4 5.8 %collective-permute-start.2 = (bf16[2,64,512]{2,1,0:T(8,128)(2,1)S(1)}, bf16[2,64,512]{2,1,0:T(8,128)(2,1)S(1)}, u32[]{:S(2)}, u32[]{:S(2)}) collective-permute-start(bf16[2,64,512]{2,1,0:T(8,128)(2,1)S(1)} %get-tuple-element.19), channel_id=1, source_target_pairs={{0,48},{16,64},{32,80},{48,96},{64,112},{80,0},{96,16},{112,32},{1... | collective-permute-start | bytes 393224 | tf_op jit(solution)/shard_map/ppermute | solution.py:63
  31.7 5.5 %collective-permute-start.3 = (bf16[2,64,512]{2,1,0:T(8,128)(2,1)S(1)}, bf16[2,64,512]{2,1,0:T(8,128)(2,1)S(1)}, u32[]{:S(2)}, u32[]{:S(2)}) collective-permute-start(bf16[2,64,512]{2,1,0:T(8,128)(2,1)S(1)} %get-tuple-element.18), channel_id=1, source_target_pairs={{0,64},{16,80},{32,96},{48,112},{64,0},{80,16},{96,32},{112,48},{1... | collective-permute-start | bytes 393224 | tf_op jit(solution)/shard_map/ppermute | solution.py:63
  32.6 10.3 %collective-permute-start.4 = (bf16[2,64,512]{2,1,0:T(8,128)(2,1)S(1)}, bf16[2,64,512]{2,1,0:T(8,128)(2,1)S(1)}, u32[]{:S(2)}, u32[]{:S(2)}) collective-permute-start(bf16[2,64,512]{2,1,0:T(8,128)(2,1)S(1)} %get-tuple-element.17), channel_id=1, source_target_pairs={{0,80},{16,96},{32,112},{48,0},{64,16},{80,32},{96,48},{112,64},{1... | collective-permute-start | bytes 393224 | tf_op jit(solution)/shard_map/ppermute | solution.py:63
  35.0 8.0 %collective-permute-start.5 = (bf16[2,64,512]{2,1,0:T(8,128)(2,1)S(1)}, bf16[2,64,512]{2,1,0:T(8,128)(2,1)S(1)}, u32[]{:S(2)}, u32[]{:S(2)}) collective-permute-start(bf16[2,64,512]{2,1,0:T(8,128)(2,1)S(1)} %get-tuple-element.16), channel_id=1, source_target_pairs={{0,96},{16,112},{32,0},{48,16},{64,32},{80,48},{96,64},{112,80},{1... | collective-permute-start | bytes 393224 | tf_op jit(solution)/shard_map/ppermute | solution.py:63
  35.9 7.2 %collective-permute-start.6 = (bf16[2,64,512]{2,1,0:T(8,128)(2,1)S(1)}, bf16[2,64,512]{2,1,0:T(8,128)(2,1)S(1)}, u32[]{:S(2)}, u32[]{:S(2)}) collective-permute-start(bf16[2,64,512]{2,1,0:T(8,128)(2,1)S(1)} %get-tuple-element.15), channel_id=1, source_target_pairs={{0,112},{16,0},{32,16},{48,32},{64,48},{80,64},{96,80},{112,96},{1... | collective-permute-start | bytes 393224 | tf_op jit(solution)/shard_map/ppermute | solution.py:63
  366.9 7.8 %collective-permute-start.7 = (bf16[2,64,512]{2,1,0:T(8,128)(2,1)S(1)}, bf16[2,64,512]{2,1,0:T(8,128)(2,1)S(1)}, u32[]{:S(2)}, u32[]{:S(2)}) collective-permute-start(bf16[2,64,512]{2,1,0:T(8,128)(2,1)S(1)} %get-tuple-element.13), channel_id=1, source_target_pairs={{0,16},{16,32},{32,48},{48,64},{64,80},{80,96},{96,112},{112,0},{1... | collective-permute-start | bytes 393224 | tf_op jit(solution)/shard_map/ppermute | solution.py:87
  368.5 7.4 %collective-permute-start.8 = (bf16[2,64,512]{2,1,0:T(8,128)(2,1)S(1)}, bf16[2,64,512]{2,1,0:T(8,128)(2,1)S(1)}, u32[]{:S(2)}, u32[]{:S(2)}) collective-permute-start(bf16[2,64,512]{2,1,0:T(8,128)(2,1)S(1)} %get-tuple-element.12), channel_id=1, source_target_pairs={{0,32},{16,48},{32,64},{48,80},{64,96},{80,112},{96,0},{112,16},{1... | collective-permute-start | bytes 393224 | tf_op jit(solution)/shard_map/ppermute | solution.py:87
  371.3 5.8 %collective-permute-start.9 = (bf16[2,64,512]{2,1,0:T(8,128)(2,1)S(1)}, bf16[2,64,512]{2,1,0:T(8,128)(2,1)S(1)}, u32[]{:S(2)}, u32[]{:S(2)}) collective-permute-start(bf16[2,64,512]{2,1,0:T(8,128)(2,1)S(1)} %get-tuple-element.11), channel_id=1, source_target_pairs={{0,48},{16,64},{32,80},{48,96},{64,112},{80,0},{96,16},{112,32},{1... | collective-permute-start | bytes 393224 | tf_op jit(solution)/shard_map/ppermute | solution.py:87
  371.3 5.8 %collective-permute-start.10 = (bf16[2,64,512]{2,1,0:T(8,128)(2,1)S(1)}, bf16[2,64,512]{2,1,0:T(8,128)(2,1)S(1)}, u32[]{:S(2)}, u32[]{:S(2)}) collective-permute-start(bf16[2,64,512]{2,1,0:T(8,128)(2,1)S(1)} %get-tuple-element.10), channel_id=1, source_target_pairs={{0,64},{16,80},{32,96},{48,112},{64,0},{80,16},{96,32},{112,48},{1... | collective-permute-start | bytes 393224 | tf_op jit(solution)/shard_map/ppermute | solution.py:87
  372.6 10.3 %collective-permute-start.11 = (bf16[2,64,512]{2,1,0:T(8,128)(2,1)S(1)}, bf16[2,64,512]{2,1,0:T(8,128)(2,1)S(1)}, u32[]{:S(2)}, u32[]{:S(2)}) collective-permute-start(bf16[2,64,512]{2,1,0:T(8,128)(2,1)S(1)} %get-tuple-element.9), channel_id=1, source_target_pairs={{0,80},{16,96},{32,112},{48,0},{64,16},{80,32},{96,48},{112,64},{1... | collective-permute-start | bytes 393224 | tf_op jit(solution)/shard_map/ppermute | solution.py:87
  374.7 8.1 %collective-permute-start.12 = (bf16[2,64,512]{2,1,0:T(8,128)(2,1)S(1)}, bf16[2,64,512]{2,1,0:T(8,128)(2,1)S(1)}, u32[]{:S(2)}, u32[]{:S(2)}) collective-permute-start(bf16[2,64,512]{2,1,0:T(8,128)(2,1)S(1)} %get-tuple-element.8), channel_id=1, source_target_pairs={{0,96},{16,112},{32,0},{48,16},{64,32},{80,48},{96,64},{112,80},{1... | collective-permute-start | bytes 393224 | tf_op jit(solution)/shard_map/ppermute | solution.py:87
  375.9 7.2 %collective-permute-start.13 = (bf16[2,64,512]{2,1,0:T(8,128)(2,1)S(1)}, bf16[2,64,512]{2,1,0:T(8,128)(2,1)S(1)}, u32[]{:S(2)}, u32[]{:S(2)}) collective-permute-start(bf16[2,64,512]{2,1,0:T(8,128)(2,1)S(1)} %get-tuple-element.7), channel_id=1, source_target_pairs={{0,112},{16,0},{32,16},{48,32},{64,48},{80,64},{96,80},{112,96},{1... | collective-permute-start | bytes 393224 | tf_op jit(solution)/shard_map/ppermute | solution.py:87
  392.4 79.3 %copy-start.1 = (bf16[320,512]{1,0:T(8,128)(2,1)S(1)}, bf16[320,512]{1,0:T(8,128)(2,1)}, u32[]{:S(2)}) copy-start(bf16[320,512]{1,0:T(8,128)(2,1)} %param.5) | copy-start | bytes 983044
Sparse Core Ops, SparseCore 0:
  392.6 79.1 reduce-scatter.3
